TPU v7x, 256 devices: a whole 4x4x8 slice. The times are simulated.
256 devices in a mesh: member: 8 (over z_hi, core), tile: 32 (over y, x, z_lo).
Axes of the slice: x: 4, y: 4, z: 8 (z_hi: 4, z_lo: 2; z = z_hi * 2 + z_lo), core: 2. Of those that a mesh axis runs over, the one named last changes fastest.
Arguments:
- upsampled_coarse: bfloat16 [128, 32, 256], P('tile'), may hold values from -6 to 6
- target: bfloat16 [128, 32, 256], P('tile'), may hold values from -6 to 6
- seeds: int32 [16], P('member'), may hold values from 0 to 63
- band_row: int32 [1], replicated, may hold values from 0 to 1920
- noise_bank: float32 [64, 16], replicated, may hold values from -5 to 5
- cond_weight: float32 [16, 256], replicated, may hold values from -1.5 to 1.5
- conv_in: bfloat16 [3, 3, 32, 128], replicated, may hold values from -0.375 to 0.375
- conv_mid: bfloat16 [3, 3, 128, 128], replicated, may hold values from -0.1875 to 0.1875
- conv_out: bfloat16 [3, 3, 128, 128], replicated, may hold values from -0.1875 to 0.1875
- head_weight: bfloat16 [128, 32], replicated, may hold values from -0.5 to 0.5
- per_quantity_offset: float32 [32], replicated, may hold values from -3 to 3
Outputs:
- crps_map: float32 [128, 32, 256], P('tile', 'member')
- conv_grad: float32 [3, 3, 128, 128], replicated
- head_grad: float32 [128, 32], replicated
- bias_grad: float32 [32], replicated
Inputs may be any that keep to these rules, and one draw needn't show every extreme that they name: `band_row`: the band lies inside the grid.
All inputs are finite; a program needn't handle non-finite values.
Results may differ from a plain program's by a relative error of at most 0.0015.
Values may be sent and summed in bfloat16 or wider, within the bound.
No kernel may reach another device: no remote copies, remote signals or barrier semaphores. Data moves between devices by JAX's collectives and lax.ppermute only.
A program may use at most 64 MiB of HBM per device.

v0:
```python
import math
import jax
import jax.numpy as jnp
from jax import lax
from jax.sharding import Mesh, PartitionSpec as P

GRID_ROWS = 2048
MEMBER = ("group", "core")


def extended(x, sides, width):
    for axis, dim in sides:
        devices, length = (lax.axis_size(axis), x.shape[dim])
        up = [(i, (i + 1) % devices) for i in range(devices - 1)]
        down = [(j, i) for i, j in up]
        before = lax.slice_in_dim(lax.ppermute(x, axis, up), length - width, length, axis=dim)
        after = lax.slice_in_dim(lax.ppermute(x, axis, down), 0, width, axis=dim)
        x = jnp.concatenate([before, x, after], axis=dim)
    return x


def input_conv(padded, kernel):
    out_rows = padded.shape[0] - 2
    col_count = padded.shape[2]
    wide = jnp.pad(padded, ((0, 0), (0, 0), (1, 1)))
    shifted = jnp.concatenate(
        [wide[i : i + out_rows, :, j : j + col_count] for i in range(3) for j in range(3)], axis=1
    )
    return jnp.einsum(
        "rkw,kc->rwc",
        shifted,
        kernel.reshape(-1, kernel.shape[3]),
        preferred_element_type=jnp.float32,
    )


def feature_conv(padded, kernel):
    out_rows = padded.shape[1] - 2
    col_count = padded.shape[2]
    wide = jnp.pad(padded, ((0, 0), (0, 0), (1, 1), (0, 0)))
    shifted = jnp.concatenate([wide[:, :, j : j + col_count] for j in range(3)], axis=3)
    summed = jnp.zeros((padded.shape[0], out_rows, col_count, kernel.shape[3]), jnp.float32)
    for i in range(3):
        summed = summed + jnp.einsum(
            "mrwc,cd->mrwd",
            shifted[:, i : i + out_rows],
            kernel[i].reshape(-1, kernel.shape[3]),
            preferred_element_type=jnp.float32,
        )
    return summed


def condition(base, cond_scale, cond_shift):
    average = jnp.mean(base, axis=-1, keepdims=True)
    centred = base - average
    spread = jnp.mean(centred * centred, axis=-1, keepdims=True)
    normed = centred * lax.rsqrt(spread + 1e-05)
    mixed = normed[None] * (1.0 + cond_scale[:, None, None, :]) + cond_shift[:, None, None, :]
    return jax.nn.gelu(mixed).astype(jnp.bfloat16)


def abs_terms(probe, sample_group_predictions):

    def abs_single(member_index):
        return jnp.sum(jnp.abs(member_index[None] - sample_group_predictions), axis=0)

    return lax.map(abs_single, probe)


def sign_terms(probe, sample_group_predictions):

    def sign_single(member_index):
        return jnp.sum(jnp.sign(member_index[None] - sample_group_predictions), axis=0)

    return lax.map(sign_single, probe)


def all_reduce_sum(parts):
    peers = ("group", "tile")
    devices = lax.axis_size("group") * lax.axis_size("tile")
    flat = jnp.concatenate([p.reshape(-1) for p in parts])
    total = flat.shape[0]
    width = -(-total // (2 * devices * 128)) * 128
    flat = jnp.pad(flat, (0, 2 * width * devices - total)).reshape(2, devices * width)
    core = lax.axis_index("core")
    swap = [(0, 1), (1, 0)]
    first = core == 0
    keep = jnp.where(first, flat[0], flat[1])
    half = keep + lax.ppermute(jnp.where(first, flat[1], flat[0]), "core", swap)
    pieces = lax.all_to_all(half.reshape(devices, width), peers, 0, 0, tiled=True)
    own = jnp.sum(pieces, axis=0, keepdims=True)
    summed = lax.all_to_all(jnp.broadcast_to(own, (devices, width)), peers, 0, 0, tiled=True)
    summed = summed.reshape(-1)
    other = lax.ppermute(summed, "core", swap)
    spread = jnp.where(first, jnp.concatenate([summed, other]), jnp.concatenate([other, summed]))
    out, at = ([], 0)
    for p in parts:
        out.append(spread[at : at + p.size].reshape(p.shape))
        at += p.size
    return tuple(out)


def on_device(
    upsampled_coarse,
    target,
    seeds,
    band_row,
    noise_bank,
    cond_weight,
    conv_in,
    conv_mid,
    conv_out,
    head_weight,
    per_quantity_offset,
):
    channels = conv_mid.shape[3]
    row_count = upsampled_coarse.shape[0]
    var_count = upsampled_coarse.shape[1]
    col_count = upsampled_coarse.shape[2]
    tile_count = lax.axis_size("tile")
    tile_at = lax.axis_index("tile")
    band_rows = row_count * tile_count
    selector = (seeds[:, None] == jnp.arange(noise_bank.shape[0], dtype=jnp.int32)[None]).astype(
        jnp.float32
    )
    noise_vec = jnp.dot(selector, noise_bank, precision=lax.Precision.HIGHEST)
    random_latent_gain = jnp.dot(noise_vec, cond_weight, precision=lax.Precision.HIGHEST)
    cond_scale = random_latent_gain[:, :channels]
    cond_shift = random_latent_gain[:, channels:]
    input_padded = extended(upsampled_coarse, (("tile", 0),), 3)
    band_at = tile_at * row_count + jnp.arange(-2, row_count + 2, dtype=jnp.int32)
    inside = ((band_at >= 0) & (band_at < band_rows))[None, :, None, None]
    first_wide = condition(input_conv(input_padded, conv_in), cond_scale, cond_shift)
    first_wide = jnp.where(inside, first_wide, jnp.zeros_like(first_wide))
    first_hidden = first_wide[:, 2 : 2 + row_count]
    second_padded = jax.nn.gelu(feature_conv(first_wide, conv_mid)).astype(jnp.bfloat16)
    second_padded = jnp.where(inside[:, 1:-1], second_padded, jnp.zeros_like(second_padded))
    final_linear_response = feature_conv(second_padded, conv_out)
    latent_layer_three = (
        first_hidden.astype(jnp.float32) + jax.nn.gelu(final_linear_response)
    ).astype(jnp.bfloat16)
    final_layer_result = jnp.einsum(
        "mrwc,cv->vmrw", latent_layer_three, head_weight, preferred_element_type=jnp.float32
    )
    sample_prediction = (
        final_layer_result
        + jnp.transpose(upsampled_coarse, (1, 0, 2)).astype(jnp.float32)[:, None]
        + per_quantity_offset[:, None, None, None]
    ).astype(jnp.bfloat16)
    row_global = band_row[0] + tile_at * row_count + jnp.arange(row_count, dtype=jnp.int32)
    latitude = math.pi * (row_global.astype(jnp.float32) + 0.5) / GRID_ROWS - math.pi / 2
    row_factor = (jnp.cos(latitude) / (band_rows * col_count))[None, None, :, None]
    var_share = var_count // (lax.axis_size("group") * lax.axis_size("core"))
    var_start = lax.axis_index(MEMBER) * var_share
    collected_members = lax.all_to_all(
        sample_prediction, MEMBER, split_axis=0, concat_axis=1, tiled=True
    )
    sample_group_predictions = collected_members.astype(jnp.float32)
    member_count = sample_group_predictions.shape[1]
    truth = jnp.transpose(
        lax.dynamic_slice_in_dim(target, var_start, var_share, 1), (1, 0, 2)
    ).astype(jnp.float32)[:, None]
    pair_differ = sample_group_predictions[:, :, None] - sample_group_predictions[:, None, :]
    abs_sums = jnp.sum(jnp.abs(pair_differ), axis=2)
    sign_sums = jnp.sum(jnp.sign(pair_differ), axis=2)
    crps_share = jnp.mean(jnp.abs(sample_group_predictions - truth), axis=1) - jnp.sum(
        abs_sums, axis=1
    ) / (2 * member_count * (member_count - 1))
    crps_map = jnp.transpose(crps_share, (1, 0, 2))
    cot_share = (
        row_factor
        * (
            jnp.sign(sample_group_predictions - truth) / member_count
            - sign_sums / (member_count * (member_count - 1))
        )
    ).astype(jnp.bfloat16)
    cotangent = lax.all_to_all(cot_share, MEMBER, split_axis=1, concat_axis=0, tiled=True)
    head_grad = jnp.einsum(
        "mrwc,vmrw->cv", latent_layer_three, cotangent, preferred_element_type=jnp.float32
    )
    bias_grad = jnp.sum(cotangent.astype(jnp.float32), axis=(1, 2, 3))
    back = jnp.einsum("vmrw,cv->mrwc", cotangent, head_weight, preferred_element_type=jnp.float32)
    unused_out, pullback = jax.vjp(jax.nn.gelu, final_linear_response)
    slope = lax.optimization_barrier(pullback(jnp.ones_like(final_linear_response))[0])
    d_pre = (back * slope).astype(jnp.bfloat16)
    second_wide = jnp.pad(second_padded, ((0, 0), (0, 0), (1, 1), (0, 0)))
    rows_of = []
    for i in range(3):
        cols_of = []
        for j in range(3):
            cols_of.append(
                jnp.einsum(
                    "mrwc,mrwd->cd",
                    second_wide[:, i : i + row_count, j : j + col_count],
                    d_pre,
                    preferred_element_type=jnp.float32,
                )
            )
        rows_of.append(jnp.stack(cols_of))
    conv_grad = jnp.stack(rows_of)
    conv_grad, head_grad_t, bias_grad = all_reduce_sum((conv_grad, head_grad.T, bias_grad))
    head_grad = head_grad_t.T
    return (crps_map, conv_grad, head_grad, bias_grad)


def solution(mesh):
    members = mesh.shape["member"]
    split = Mesh(
        mesh.devices.reshape(members // 2, 2, mesh.shape["tile"]), ("group", "core", "tile")
    )
    return jax.shard_map(
        on_device,
        mesh=split,
        in_specs=(
            P("tile", None, None),
            P("tile", None, None),
            P(MEMBER),
            P(),
            P(),
            P(),
            P(),
            P(),
            P(),
            P(),
            P(),
        ),
        out_specs=(P("tile", MEMBER, None), P(), P(), P()),
        check_vma=False,
    )
```

profile of v0, /device:TPU:1, one launch (start us, length us, event | category | flops | bytes accessed | tf_op | source)
XLA Modules:
  0.0 115.7 jit_solution(1448701602072918489)
XLA Ops:
  0.7 4.5 %collective-permute-start = (bf16[4,32,256]{2,1,0:T(8,128)(2,1)}, bf16[4,32,256]{2,1,0:T(8,128)(2,1)S(1)}, u32[]{:S(2)}, u32[]{:S(2)}) collective-permute-start(bf16[4,32,256]{2,1,0:T(8,128)(2,1)} %param.11), channel_id=1, source_target_pairs={{0,1},{1,2},{2,3},{3,4},{4,5},{5,6},{6,7},{7,8},{8,9},{9,10},{10,1... | collective-permute-start | bytes 196616 | tf_op jit(solution)/shard_map/ppermute | solution.py:16
  5.2 1.3 %collective-permute-start.1 = (bf16[4,32,256]{2,1,0:T(8,128)(2,1)}, bf16[4,32,256]{2,1,0:T(8,128)(2,1)S(1)}, u32[]{:S(2)}, u32[]{:S(2)}) collective-permute-start(bf16[4,32,256]{2,1,0:T(8,128)(2,1)} %param.11), channel_id=1, source_target_pairs={{1,0},{2,1},{3,2},{4,3},{5,4},{6,5},{7,6},{8,7},{9,8},{10,9},{11,1... | collective-permute-start | bytes 196616 | tf_op jit(solution)/shard_map/ppermute | solution.py:17
  6.5 0.9 convert_bitcast_fusion
  7.3 0.9 fusion.54
  8.2 0.8 fusion.70
  9.1 1.0 fusion.68
  10.2 1.0 fusion.67
  13.1 0.9 fusion.23
  14.6 0.8 fusion.65
  15.4 0.8 fusion.66
  16.2 1.2 %fusion.22 = bf16[2,6,256,128]{3,2,1,0:T(8,128)(2,1)S(1)} fusion(bf16[384,128,1,1]{1,0,3,2:T(8,128)(2,1)S(1)} %bitcast.189, f32[2,6,256,128]{3,2,1,0:T(8,128)S(1)} %fusion.66, f32[2,6,256,128]{3,2,1,0:T(8,128)S(1)} %fusion.65, pred[6]{0:T(512)(128)(4,1)S(1)} %slice_bitcast_fusion, bf16[2,8,256,128]{3,2,1,0:T(8,128)(2,1)S(1)} %get-tuple-element.21, ...), kind=kOutput, calls=%fused_computation.44 | convolution fusion | flops 316145664 | bytes 7176198 | tf_op jit(solution)/shard_map/mrwc,cd->mrwd/dot_general | solution.py:44
  19.0 1.4 %fusion.29 = (f32[2,4,256,128]{3,2,1,0:T(8,128)S(1)}, bf16[2,4,256,128]{3,2,1,0:T(8,128)(2,1)S(1)}) fusion(bf16[2,8,256,128]{3,2,1,0:T(8,128)(2,1)S(1)} %fusion.23, f32[2,4,256,128]{3,2,1,0:T(8,128)S(1)} %convolution_add_fusion.1, bf16[384,128,1,1]{1,0,3,2:T(8,128)(2,1)S(1)} %bitcast.186, bf16[2,6,256,128]{3,2,1,0:T(8,128)(2,1)S(1)} %get-tuple-element.23, ...), kind=kOutput, calls=%fused_computation.51 | convolution fusion | flops 214171648 | bytes 5603328 | tf_op jit(solution)/shard_map/mrwc,cd->mrwd/dot_general | solution.py:44
  20.7 0.8 copy.97
  21.5 8.8 %all-to-all-start = ((bf16[32,2,4,256]{3,2,1,0:T(4,128)(2,1)}), bf16[32,2,4,256]{3,2,1,0:T(4,128)(2,1)S(1)}, u32[]{:S(2)}, u32[]{:S(2)}) async-start(bf16[32,2,4,256]{3,2,1,0:T(4,128)(2,1)} %copy.97), calls=%async_computation | async-start | bytes 262144 | tf_op jit(solution)/shard_map/all_to_all | solution.py:155
  31.6 6.9 %all-to-all-done = bf16[32,2,4,256]{3,2,1,0:T(4,128)(2,1)S(1)} async-done(((bf16[32,2,4,256]{3,2,1,0:T(4,128)(2,1)}), bf16[32,2,4,256]{3,2,1,0:T(4,128)(2,1)S(1)}, u32[]{:S(2)}, u32[]{:S(2)}) %all-to-all-start) | async-done | bytes 131104 | tf_op jit(solution)/shard_map/all_to_all | solution.py:155
  38.6 2.3 %fusion.1 = (f32[4,16,4,256]{3,2,1,0:T(4,128)S(1)}, f32[4,4,256]{2,1,0:T(4,128)S(1)}) fusion(f32[4,16,4,256]{3,1,2,0:T(8,128)S(1)} %copy.100, f32[4,16,4,256]{3,2,1,0:T(4,128)S(1)} %bitcast.175), kind=kLoop, calls=%fused_computation.3 | loop fusion | flops 5173248 | bytes 802816 | tf_op jit(solution)/shard_map/reduce_sum | solution.py:165
  41.9 4.3 %all-to-all-start.1 = ((bf16[4,16,4,256]{3,2,0,1:T(4,128)(2,1)}), bf16[4,16,4,256]{3,2,0,1:T(4,128)(2,1)S(1)}, u32[]{:S(2)}, u32[]{:S(2)}) async-start(bf16[4,16,4,256]{3,2,0,1:T(4,128)(2,1)} %copy.102), calls=%async_computation.1 | async-start | bytes 262144 | tf_op jit(solution)/shard_map/all_to_all | solution.py:177
  46.2 8.7 %all-to-all-done.1 = bf16[4,16,4,256]{3,2,0,1:T(4,128)(2,1)S(1)} async-done(((bf16[4,16,4,256]{3,2,0,1:T(4,128)(2,1)}), bf16[4,16,4,256]{3,2,0,1:T(4,128)(2,1)S(1)}, u32[]{:S(2)}, u32[]{:S(2)}) %all-to-all-start.1) | async-done | bytes 131104 | tf_op jit(solution)/shard_map/all_to_all | solution.py:177
  59.3 1.3 %collective-permute-start.2 = (f32[81920]{0:T(1024)S(1)}, f32[81920]{0:T(1024)S(1)}, u32[]{:S(2)}, u32[]{:S(2)}) collective-permute-start(f32[81920]{0:T(1024)S(1)} %slice_select_fusion), channel_id=1, source_target_pairs={{0,32},{32,0},{1,33},{33,1},{2,34},{34,2},{3,35},{35,3},{4,36},{36... | collective-permute-start | bytes 983048 | tf_op jit(solution)/shard_map/ppermute | solution.py:89
  60.6 1.3 %collective-permute-done.2 = f32[81920]{0:T(1024)S(1)} collective-permute-done((f32[81920]{0:T(1024)S(1)}, f32[81920]{0:T(1024)S(1)}, u32[]{:S(2)}, u32[]{:S(2)}) %collective-permute-start.2) | collective-permute-done | bytes 327712 | tf_op jit(solution)/shard_map/ppermute | solution.py:89
  61.9 27.0 %all_to_all.42 = f32[128,1,640]{2,1,0:T(1,128)S(1)} all-to-all(f32[128,1,640]{2,1,0:T(1,128)S(1)} %bitcast.181), channel_id=1, replica_groups=mesh['group'=4,'core'=2,'tile'=32] {'group','tile'}, dimensions={0} | all-to-all | bytes 655360 | tf_op jit(solution)/shard_map/all_to_all | solution.py:90
  89.3 19.7 %all_to_all.43 = f32[128,1,640]{2,1,0:T(1,128)S(1)} all-to-all(f32[128,1,640]{2,1,0:T(1,128)S(1)} %broadcast_in_dim.29), channel_id=1, replica_groups=mesh['group'=4,'core'=2,'tile'=32] {'group','tile'}, dimensions={0} | all-to-all | bytes 655360 | tf_op jit(solution)/shard_map/all_to_all | solution.py:92
  109.0 3.4 %collective-permute-start.3 = (f32[81920]{0:T(1024)S(1)}, f32[81920]{0:T(1024)S(1)}, u32[]{:S(2)}, u32[]{:S(2)}) collective-permute-start(f32[81920]{0:T(1024)S(1)} %bitcast.177), channel_id=1, source_target_pairs={{0,32},{32,0},{1,33},{33,1},{2,34},{34,2},{3,35},{35,3},{4,36},{36... | collective-permute-start | bytes 983048 | tf_op jit(solution)/shard_map/ppermute | solution.py:94
  113.7 0.9 slice.204
  (76 shorter events, 13.3 us)
Async XLA Ops:
  0.6 11.4 %copy-start = (bf16[3,3,32,128]{3,2,1,0:T(8,128)(2,1)S(1)}, bf16[3,3,32,128]{3,2,1,0:T(8,128)(2,1)}, u32[]{:S(2)}) copy-start(bf16[3,3,32,128]{3,2,1,0:T(8,128)(2,1)} %param.17) | copy-start | bytes 221188
  0.6 10.6 %copy-start.1 = (bf16[4,32,256]{2,1,0:T(8,128)(2,1)S(1)}, bf16[4,32,256]{2,1,0:T(8,128)(2,1)}, u32[]{:S(2)}) copy-start(bf16[4,32,256]{2,1,0:T(8,128)(2,1)} %param.11) | copy-start | bytes 196612
  0.7 10.6 %collective-permute-start = (bf16[4,32,256]{2,1,0:T(8,128)(2,1)}, bf16[4,32,256]{2,1,0:T(8,128)(2,1)S(1)}, u32[]{:S(2)}, u32[]{:S(2)}) collective-permute-start(bf16[4,32,256]{2,1,0:T(8,128)(2,1)} %param.11), channel_id=1, source_target_pairs={{0,1},{1,2},{2,3},{3,4},{4,5},{5,6},{6,7},{7,8},{8,9},{9,10},{10,1... | collective-permute-start | bytes 196616 | tf_op jit(solution)/shard_map/ppermute | solution.py:16
  5.2 6.1 %collective-permute-start.1 = (bf16[4,32,256]{2,1,0:T(8,128)(2,1)}, bf16[4,32,256]{2,1,0:T(8,128)(2,1)S(1)}, u32[]{:S(2)}, u32[]{:S(2)}) collective-permute-start(bf16[4,32,256]{2,1,0:T(8,128)(2,1)} %param.11), channel_id=1, source_target_pairs={{1,0},{2,1},{3,2},{4,3},{5,4},{6,5},{7,6},{8,7},{9,8},{10,9},{11,1... | collective-permute-start | bytes 196616 | tf_op jit(solution)/shard_map/ppermute | solution.py:17
  19.0 1.4 %copy-start.2 = (bf16[128,32]{0,1:T(8,128)(2,1)S(1)}, bf16[128,32]{0,1:T(8,128)(2,1)}, u32[]{:S(2)}) copy-start(bf16[128,32]{0,1:T(8,128)(2,1)} %param.20) | copy-start | bytes 24580
  19.0 1.4 %copy-start.3 = (f32[32]{0:T(128)S(1)}, f32[32]{0:T(128)}, u32[]{:S(2)}) copy-start(f32[32]{0:T(128)} %param.21) | copy-start | bytes 388
  21.5 17.1 %all-to-all-start = ((bf16[32,2,4,256]{3,2,1,0:T(4,128)(2,1)}), bf16[32,2,4,256]{3,2,1,0:T(4,128)(2,1)S(1)}, u32[]{:S(2)}, u32[]{:S(2)}) async-start(bf16[32,2,4,256]{3,2,1,0:T(4,128)(2,1)} %copy.97), calls=%async_computation | async-start | bytes 262144 | tf_op jit(solution)/shard_map/all_to_all | solution.py:155
  41.9 13.1 %all-to-all-start.1 = ((bf16[4,16,4,256]{3,2,0,1:T(4,128)(2,1)}), bf16[4,16,4,256]{3,2,0,1:T(4,128)(2,1)S(1)}, u32[]{:S(2)}, u32[]{:S(2)}) async-start(bf16[4,16,4,256]{3,2,0,1:T(4,128)(2,1)} %copy.102), calls=%async_computation.1 | async-start | bytes 262144 | tf_op jit(solution)/shard_map/all_to_all | solution.py:177
  59.3 2.6 %collective-permute-start.2 = (f32[81920]{0:T(1024)S(1)}, f32[81920]{0:T(1024)S(1)}, u32[]{:S(2)}, u32[]{:S(2)}) collective-permute-start(f32[81920]{0:T(1024)S(1)} %slice_select_fusion), channel_id=1, source_target_pairs={{0,32},{32,0},{1,33},{33,1},{2,34},{34,2},{3,35},{35,3},{4,36},{36... | collective-permute-start | bytes 983048 | tf_op jit(solution)/shard_map/ppermute | solution.py:89
  109.0 4.6 %collective-permute-start.3 = (f32[81920]{0:T(1024)S(1)}, f32[81920]{0:T(1024)S(1)}, u32[]{:S(2)}, u32[]{:S(2)}) collective-permute-start(f32[81920]{0:T(1024)S(1)} %bitcast.177), channel_id=1, source_target_pairs={{0,32},{32,0},{1,33},{33,1},{2,34},{34,2},{3,35},{35,3},{4,36},{36... | collective-permute-start | bytes 983048 | tf_op jit(solution)/shard_map/ppermute | solution.py:94
where the time goes:
time: 116 us
  blocking collectives  46.7 us (40%)
  starting transfers between devices  23.6 us (20%)
  waiting for transfers between devices  17.4 us (15%)
  matrix products  11.4 us (10%)
  local copies, waits for them, and re-layouts  8.12 us (7%)
  other arithmetic  6.7 us (6%)
  between operations  1.76 us (2%)
    all_to_all x1, blocking collectives, all_reduce_sum(): lax.all_to_all(half.reshape(devices, width), peers, 0, 0, tiled=True)  27 us
    all_to_all x1, blocking collectives, all_reduce_sum(): lax.all_to_all(jnp.broadcast_to(own, (devices, width)), peers, 0, 0, tile...  19.7 us
    all_to_all x1, starting transfers between devices, on_device(): lax.all_to_all(sample_prediction, MEMBER, split_axis=0, concat_axis=1, ti...  8.75 us
    all_to_all x1, waiting for transfers between devices, on_device(): lax.all_to_all(cot_share, MEMBER, split_axis=1, concat_axis=0, tiled=True)  8.71 us
    all_to_all x1, waiting for transfers between devices, on_device(): lax.all_to_all(sample_prediction, MEMBER, split_axis=0, concat_axis=1, ti...  6.9 us
    dot_general x6, matrix products, feature_conv(): jnp.einsum('mrwc,cd->mrwd', shifted[:, i:i + out_rows], kernel[i].reshape...  5.26 us
    ppermute x1, starting transfers between devices, extended(): lax.ppermute(x, axis, up)  4.49 us
    all_to_all x1, starting transfers between devices, on_device(): lax.all_to_all(cot_share, MEMBER, split_axis=1, concat_axis=0, tiled=True)  4.35 us
  transfers between devices with their start and end apart: 6, of which 4 were waited for; matrix products, arithmetic and copies ran while one was open for 5% of the time, Pallas kernels for 0%

commit v1 on v0

--- a/solution.py
+++ b/solution.py
@@ -152,8 +152,11 @@
     row_factor = (jnp.cos(latitude) / (band_rows * col_count))[None, None, :, None]
     var_share = var_count // (lax.axis_size("group") * lax.axis_size("core"))
     var_start = lax.axis_index(MEMBER) * var_share
-    collected_members = lax.all_to_all(
-        sample_prediction, MEMBER, split_axis=0, concat_axis=1, tiled=True
+    collected_members = jnp.concatenate(
+        lax.all_to_all(
+            jnp.stack(jnp.split(sample_prediction, lax.axis_size(MEMBER), axis=0)), MEMBER, 0, 0
+        ),
+        axis=1,
     )
     sample_group_predictions = collected_members.astype(jnp.float32)
     member_count = sample_group_predictions.shape[1]

time: 116 us -> 121 us (1.043)
  local copies, waits for them, and re-layouts: 8.12 us -> 11.7 us
    unnamed x17 -> x23, local copies, waits for them, and re-layouts: 1.19 us -> 4.88 us
where the time goes in v1:
time: 121 us; the launch traced here: 120 us
  blocking collectives  46.7 us (39%)
  starting transfers between devices  23.6 us (20%)
  waiting for transfers between devices  17.4 us (14%)
  local copies, waits for them, and re-layouts  11.7 us (10%)
  matrix products  11.4 us (9%)
  other arithmetic  7.28 us (6%)
  between operations  1.76 us (1%)
    all_to_all x1, blocking collectives, all_reduce_sum(): lax.all_to_all(half.reshape(devices, width), peers, 0, 0, tiled=True)  27 us
    all_to_all x1, blocking collectives, all_reduce_sum(): lax.all_to_all(jnp.broadcast_to(own, (devices, width)), peers, 0, 0, tile...  19.7 us
    all_to_all x1, starting transfers between devices, on_device(): lax.all_to_all(jnp.stack(jnp.split(sample_prediction, lax.axis_size(MEMBE...  8.75 us
    all_to_all x1, waiting for transfers between devices, on_device(): lax.all_to_all(cot_share, MEMBER, split_axis=1, concat_axis=0, tiled=True)  8.71 us
    all_to_all x1, waiting for transfers between devices, on_device(): lax.all_to_all(jnp.stack(jnp.split(sample_prediction, lax.axis_size(MEMBE...  6.9 us
    dot_general x6, matrix products, feature_conv(): jnp.einsum('mrwc,cd->mrwd', shifted[:, i:i + out_rows], kernel[i].reshape...  5.26 us
    unnamed x23, local copies, waits for them, and re-layouts  4.88 us
    ppermute x1, starting transfers between devices, extended(): lax.ppermute(x, axis, up)  4.49 us
  transfers between devices with their start and end apart: 6, of which 4 were waited for; matrix products, arithmetic and copies ran while one was open for 5% of the time, Pallas kernels for 0%

profile of v1, /device:TPU:1, one launch (start us, length us, event | category | flops | bytes accessed | tf_op | source)
XLA Modules:
  0.0 119.8 jit_solution(1149089941668372214)
XLA Ops:
  0.7 4.5 %collective-permute-start = (bf16[4,32,256]{2,1,0:T(8,128)(2,1)}, bf16[4,32,256]{2,1,0:T(8,128)(2,1)S(1)}, u32[]{:S(2)}, u32[]{:S(2)}) collective-permute-start(bf16[4,32,256]{2,1,0:T(8,128)(2,1)} %param.11), channel_id=1, source_target_pairs={{0,1},{1,2},{2,3},{3,4},{4,5},{5,6},{6,7},{7,8},{8,9},{9,10},{10,1... | collective-permute-start | bytes 196616 | tf_op jit(solution)/shard_map/ppermute | solution.py:16
  5.2 1.3 %collective-permute-start.1 = (bf16[4,32,256]{2,1,0:T(8,128)(2,1)}, bf16[4,32,256]{2,1,0:T(8,128)(2,1)S(1)}, u32[]{:S(2)}, u32[]{:S(2)}) collective-permute-start(bf16[4,32,256]{2,1,0:T(8,128)(2,1)} %param.11), channel_id=1, source_target_pairs={{1,0},{2,1},{3,2},{4,3},{5,4},{6,5},{7,6},{8,7},{9,8},{10,9},{11,1... | collective-permute-start | bytes 196616 | tf_op jit(solution)/shard_map/ppermute | solution.py:17
  6.5 0.9 convert_bitcast_fusion
  7.3 0.9 fusion.59
  8.2 0.8 fusion.75
  9.1 1.0 fusion.73
  10.2 1.0 fusion.72
  13.1 0.9 fusion.23
  14.6 0.8 fusion.70
  15.4 0.8 fusion.71
  16.2 1.2 fusion.22
  19.0 1.4 %fusion.29 = (f32[2,4,256,128]{3,2,1,0:T(8,128)S(1)}, bf16[2,4,256,128]{3,2,1,0:T(8,128)(2,1)S(1)}) fusion(bf16[2,8,256,128]{3,2,1,0:T(8,128)(2,1)S(1)} %fusion.23, f32[2,4,256,128]{3,2,1,0:T(8,128)S(1)} %convolution_add_fusion.1, bf16[384,128,1,1]{1,0,3,2:T(8,128)(2,1)S(1)} %bitcast.217, bf16[2,6,256,128]{3,2,1,0:T(8,128)(2,1)S(1)} %get-tuple-element.15, ...), kind=kOutput, calls=%fused_computation.51 | convolution fusion | flops 214171648 | bytes 5603328 | tf_op jit(solution)/shard_map/mrwc,cd->mrwd/dot_general | solution.py:44
  25.6 8.8 %all-to-all-start = ((bf16[8,4,2,4,256]{4,1,3,2,0:T(4,128)(2,1)}), bf16[8,4,2,4,256]{4,1,3,2,0:T(4,128)(2,1)S(1)}, u32[]{:S(2)}, u32[]{:S(2)}) async-start(bf16[8,4,2,4,256]{4,1,3,2,0:T(4,128)(2,1)} %constant_dynamic-update-slice_fusion), calls=%async_computation | async-start | bytes 262144 | tf_op jit(solution)/shard_map/all_to_all | solution.py:156
  35.8 6.9 %all-to-all-done = bf16[8,4,2,4,256]{4,1,3,2,0:T(4,128)(2,1)S(1)} async-done(((bf16[8,4,2,4,256]{4,1,3,2,0:T(4,128)(2,1)}), bf16[8,4,2,4,256]{4,1,3,2,0:T(4,128)(2,1)S(1)}, u32[]{:S(2)}, u32[]{:S(2)}) %all-to-all-start) | async-done | bytes 131104 | tf_op jit(solution)/shard_map/all_to_all | solution.py:156
  43.0 2.3 %fusion.1 = (f32[4,16,4,256]{3,2,1,0:T(4,128)S(1)}, f32[4,4,256]{2,1,0:T(4,128)S(1)}) fusion(f32[4,16,4,256]{3,1,2,0:T(8,128)S(1)} %copy.132, f32[4,16,4,256]{3,2,1,0:T(4,128)S(1)} %copy.90), kind=kLoop, calls=%fused_computation.3 | loop fusion | flops 5173248 | bytes 802816 | tf_op jit(solution)/shard_map/reduce_sum | solution.py:168
  45.5 0.7 copy.94
  46.2 4.3 %all-to-all-start.1 = ((bf16[4,16,4,256]{3,2,0,1:T(4,128)(2,1)}), bf16[4,16,4,256]{3,2,0,1:T(4,128)(2,1)S(1)}, u32[]{:S(2)}, u32[]{:S(2)}) async-start(bf16[4,16,4,256]{3,2,0,1:T(4,128)(2,1)} %copy.94), calls=%async_computation.1 | async-start | bytes 262144 | tf_op jit(solution)/shard_map/all_to_all | solution.py:180
  50.6 8.7 %all-to-all-done.1 = bf16[4,16,4,256]{3,2,0,1:T(4,128)(2,1)S(1)} async-done(((bf16[4,16,4,256]{3,2,0,1:T(4,128)(2,1)}), bf16[4,16,4,256]{3,2,0,1:T(4,128)(2,1)S(1)}, u32[]{:S(2)}, u32[]{:S(2)}) %all-to-all-start.1) | async-done | bytes 131104 | tf_op jit(solution)/shard_map/all_to_all | solution.py:180
  63.4 1.3 %collective-permute-start.2 = (f32[81920]{0:T(1024)S(1)}, f32[81920]{0:T(1024)S(1)}, u32[]{:S(2)}, u32[]{:S(2)}) collective-permute-start(f32[81920]{0:T(1024)S(1)} %slice_select_fusion), channel_id=1, source_target_pairs={{0,32},{32,0},{1,33},{33,1},{2,34},{34,2},{3,35},{35,3},{4,36},{36... | collective-permute-start | bytes 983048 | tf_op jit(solution)/shard_map/ppermute | solution.py:89
  64.7 1.3 %collective-permute-done.2 = f32[81920]{0:T(1024)S(1)} collective-permute-done((f32[81920]{0:T(1024)S(1)}, f32[81920]{0:T(1024)S(1)}, u32[]{:S(2)}, u32[]{:S(2)}) %collective-permute-start.2) | collective-permute-done | bytes 327712 | tf_op jit(solution)/shard_map/ppermute | solution.py:89
  66.1 27.0 %all_to_all.38 = f32[128,1,640]{2,1,0:T(1,128)S(1)} all-to-all(f32[128,1,640]{2,1,0:T(1,128)S(1)} %bitcast.212), channel_id=1, replica_groups=mesh['group'=4,'core'=2,'tile'=32] {'group','tile'}, dimensions={0} | all-to-all | bytes 655360 | tf_op jit(solution)/shard_map/all_to_all | solution.py:90
  93.4 19.7 %all_to_all.39 = f32[128,1,640]{2,1,0:T(1,128)S(1)} all-to-all(f32[128,1,640]{2,1,0:T(1,128)S(1)} %broadcast_in_dim.29), channel_id=1, replica_groups=mesh['group'=4,'core'=2,'tile'=32] {'group','tile'}, dimensions={0} | all-to-all | bytes 655360 | tf_op jit(solution)/shard_map/all_to_all | solution.py:92
  113.2 3.4 %collective-permute-start.3 = (f32[81920]{0:T(1024)S(1)}, f32[81920]{0:T(1024)S(1)}, u32[]{:S(2)}, u32[]{:S(2)}) collective-permute-start(f32[81920]{0:T(1024)S(1)} %bitcast.208), channel_id=1, source_target_pairs={{0,32},{32,0},{1,33},{33,1},{2,34},{34,2},{3,35},{35,3},{4,36},{36... | collective-permute-start | bytes 983048 | tf_op jit(solution)/shard_map/ppermute | solution.py:94
  117.9 0.9 slice.204
  (80 shorter events, 17.5 us)
Async XLA Ops:
  0.6 11.4 %copy-start = (bf16[3,3,32,128]{3,2,1,0:T(8,128)(2,1)S(1)}, bf16[3,3,32,128]{3,2,1,0:T(8,128)(2,1)}, u32[]{:S(2)}) copy-start(bf16[3,3,32,128]{3,2,1,0:T(8,128)(2,1)} %param.17) | copy-start | bytes 221188
  0.6 10.6 %copy-start.1 = (bf16[4,32,256]{2,1,0:T(8,128)(2,1)S(1)}, bf16[4,32,256]{2,1,0:T(8,128)(2,1)}, u32[]{:S(2)}) copy-start(bf16[4,32,256]{2,1,0:T(8,128)(2,1)} %param.11) | copy-start | bytes 196612
  0.7 10.6 %collective-permute-start = (bf16[4,32,256]{2,1,0:T(8,128)(2,1)}, bf16[4,32,256]{2,1,0:T(8,128)(2,1)S(1)}, u32[]{:S(2)}, u32[]{:S(2)}) collective-permute-start(bf16[4,32,256]{2,1,0:T(8,128)(2,1)} %param.11), channel_id=1, source_target_pairs={{0,1},{1,2},{2,3},{3,4},{4,5},{5,6},{6,7},{7,8},{8,9},{9,10},{10,1... | collective-permute-start | bytes 196616 | tf_op jit(solution)/shard_map/ppermute | solution.py:16
  5.2 6.1 %collective-permute-start.1 = (bf16[4,32,256]{2,1,0:T(8,128)(2,1)}, bf16[4,32,256]{2,1,0:T(8,128)(2,1)S(1)}, u32[]{:S(2)}, u32[]{:S(2)}) collective-permute-start(bf16[4,32,256]{2,1,0:T(8,128)(2,1)} %param.11), channel_id=1, source_target_pairs={{1,0},{2,1},{3,2},{4,3},{5,4},{6,5},{7,6},{8,7},{9,8},{10,9},{11,1... | collective-permute-start | bytes 196616 | tf_op jit(solution)/shard_map/ppermute | solution.py:17
  19.0 1.4 %copy-start.2 = (bf16[128,32]{0,1:T(8,128)(2,1)S(1)}, bf16[128,32]{0,1:T(8,128)(2,1)}, u32[]{:S(2)}) copy-start(bf16[128,32]{0,1:T(8,128)(2,1)} %param.20) | copy-start | bytes 24580
  19.0 1.4 %copy-start.3 = (f32[32]{0:T(128)S(1)}, f32[32]{0:T(128)}, u32[]{:S(2)}) copy-start(f32[32]{0:T(128)} %param.21) | copy-start | bytes 388
  25.6 17.1 %all-to-all-start = ((bf16[8,4,2,4,256]{4,1,3,2,0:T(4,128)(2,1)}), bf16[8,4,2,4,256]{4,1,3,2,0:T(4,128)(2,1)S(1)}, u32[]{:S(2)}, u32[]{:S(2)}) async-start(bf16[8,4,2,4,256]{4,1,3,2,0:T(4,128)(2,1)} %constant_dynamic-update-slice_fusion), calls=%async_computation | async-start | bytes 262144 | tf_op jit(solution)/shard_map/all_to_all | solution.py:156
  46.2 13.1 %all-to-all-start.1 = ((bf16[4,16,4,256]{3,2,0,1:T(4,128)(2,1)}), bf16[4,16,4,256]{3,2,0,1:T(4,128)(2,1)S(1)}, u32[]{:S(2)}, u32[]{:S(2)}) async-start(bf16[4,16,4,256]{3,2,0,1:T(4,128)(2,1)} %copy.94), calls=%async_computation.1 | async-start | bytes 262144 | tf_op jit(solution)/shard_map/all_to_all | solution.py:180
  63.4 2.6 %collective-permute-start.2 = (f32[81920]{0:T(1024)S(1)}, f32[81920]{0:T(1024)S(1)}, u32[]{:S(2)}, u32[]{:S(2)}) collective-permute-start(f32[81920]{0:T(1024)S(1)} %slice_select_fusion), channel_id=1, source_target_pairs={{0,32},{32,0},{1,33},{33,1},{2,34},{34,2},{3,35},{35,3},{4,36},{36... | collective-permute-start | bytes 983048 | tf_op jit(solution)/shard_map/ppermute | solution.py:89
  113.2 4.6 %collective-permute-start.3 = (f32[81920]{0:T(1024)S(1)}, f32[81920]{0:T(1024)S(1)}, u32[]{:S(2)}, u32[]{:S(2)}) collective-permute-start(f32[81920]{0:T(1024)S(1)} %bitcast.208), channel_id=1, source_target_pairs={{0,32},{32,0},{1,33},{33,1},{2,34},{34,2},{3,35},{35,3},{4,36},{36... | collective-permute-start | bytes 983048 | tf_op jit(solution)/shard_map/ppermute | solution.py:94
